TPU v7x, 512 devices: a whole 4x4x16 slice. The times are simulated.
512 devices in a mesh: seg: 32 (over z, core), row: 16 (over x, y).
Axes of the slice: x: 4, y: 4, z: 16, core: 2. Of those that a mesh axis runs over, the one named last changes fastest.
Arguments:
- basis: bfloat16 [32, 8192, 1024], P('seg', 'row'), may hold values from -6 to 6
- arriving: bfloat16 [8192, 1024], P('row'), may hold values from -6 to 6
- blocks: bfloat16 [32, 8192, 256], P('seg', 'row'), may hold values from -8 to 8
- pattern: int32 [32, 128, 4], P('seg', 'row'), may hold values from 0 to 127, as said below
- growth: float32 [32, 1024], P('seg'), may hold values from -6 to 6
Outputs:
- next_basis: bfloat16 [32, 8192, 1024], P('seg', 'row')
- next_growth: float32 [32, 1024], P('seg')
Inputs may be any that keep to these rules, and one draw needn't show every extreme that they name: `pattern`: entry 0 of block row r is r itself; entry 1 is the block 4 positions before or after r on the cycle of 128 blocks; the other entries are distinct blocks fewer than 4 positions from r and not r.
All inputs are finite; a program needn't handle non-finite values.
Results may differ from a plain program's by a relative error of at most 0.0053.
Values may be sent and summed in bfloat16 or wider, within the bound.
No kernel may reach another device: no remote copies, remote signals or barrier semaphores. Data moves between devices by JAX's collectives and lax.ppermute only.
A program may use at most 128 MiB of HBM per device.

v0:
```python
import jax
import jax.numpy as jnp
from jax import lax
from jax.sharding import PartitionSpec as P

BS = 64
NB = 4
REACH = 4


def padded_2(block, sides, width):
    for axis, dim in sides:
        count = lax.axis_size(axis)
        forward = [(i, i + 1) for i in range(count - 1)]
        forward.append((count - 1, 0))
        backward = [(target, source) for source, target in forward]
        low = lax.ppermute(
            lax.slice_in_dim(block, block.shape[dim] - width, None, axis=dim), axis, forward
        )
        high = lax.ppermute(lax.slice_in_dim(block, 0, width, axis=dim), axis, backward)
        block = jnp.concatenate([low, block, high], axis=dim)
    return block


def shifted(array, axis, by):
    length = lax.axis_size(axis)
    pairs = [(i, i + by) for i in range(length) if 0 <= i + by < length]
    return lax.ppermute(array, axis, pairs)


def body(basis, arriving, blocks, pattern, growth):
    row_count = basis.shape[1]
    col_count = basis.shape[2]
    row_blocks = row_count // BS
    total_blocks = row_blocks * lax.axis_size("row")
    padded = padded_2(basis[0], (("row", 0),), REACH * BS)
    tile_stack = padded.reshape(row_blocks + 2 * REACH, BS, col_count)
    local_ids = jnp.arange(row_blocks, dtype=jnp.int32)
    own_blocks = lax.axis_index("row") * row_blocks + local_ids
    offsets = (pattern[0] - own_blocks[:, None] + REACH) % total_blocks
    picked = jnp.take(tile_stack, local_ids[:, None] + offsets, axis=0)
    values = blocks[0].reshape(row_blocks, BS, NB, BS)
    propagated = jnp.einsum("rinj,rnjk->rik", values, picked, preferred_element_type=jnp.float32)
    propagated = propagated.reshape(row_count, col_count).astype(jnp.bfloat16)
    partial_value = lax.dot_general(
        propagated, propagated, (((0,), (0,)), ((), ())), preferred_element_type=jnp.float32
    )
    gram_matrix = lax.psum(partial_value, "row")
    gram_matrix = gram_matrix / (row_count * lax.axis_size("row"))
    factor = jnp.linalg.cholesky(gram_matrix)
    next_growth = growth + jnp.log(jnp.diagonal(factor))[None, :]
    wide_rows = propagated.astype(jnp.float32)
    first_section = lax.axis_index("seg") == 0
    renewed = lax.linalg.triangular_solve(
        factor, wide_rows, left_side=False, lower=True, transpose_a=True
    )
    received = shifted(renewed.astype(jnp.bfloat16)[None], "seg", 1)
    next_basis = jnp.where(first_section, arriving[None], received)
    return (next_basis, next_growth)


def solution(mesh):
    return jax.shard_map(
        body,
        mesh=mesh,
        in_specs=(
            P("seg", "row", None),
            P("row", None),
            P("seg", "row", None),
            P("seg", "row", None),
            P("seg", None),
        ),
        out_specs=(P("seg", "row", None), P("seg", None)),
        check_vma=False,
    )
```

profile of v0, /device:TPU:1, one launch (start us, length us, event | category | flops | bytes accessed | tf_op | source)
XLA Modules:
  0.0 577.8 jit_solution(9313028965769077689)
XLA Ops:
  12.5 5.6 collective-permute-start.1
  35.5 143.7 %all-reduce.3.cloned.1.call-done = f32[1024,1024]{0,1:T(8,128)} async-done(((f32[1024,1024]{0,1:T(8,128)}), f32[1024,1024]{0,1:T(8,128)}) %all-reduce.3.cloned.1.call-update) | async-done | bytes 4194320 | tf_op jit(solution)/shard_map/psum | solution.py:48
  179.2 5.0 broadcast_multiply_fusion
  184.2 5.8 %copy.19 = f32[1024,1024]{1,0:T(8,128)} copy(f32[1024,1024]{0,1:T(8,128)} %broadcast_multiply_fusion) | data formatting | bytes 8388608 | tf_op jit(solution)/shard_map/div | solution.py:49
  190.0 4.4 fusion
  196.4 11.7 %cholesky.223 = f32[128,128]{1,0:T(8,128)S(1)} custom-call(f32[128,128]{1,0:T(8,128)S(1)} %cholesky.580), custom_call_target="Cholesky" | custom-call | tf_op jit(solution)/shard_map/jit(cholesky)/cholesky | solution.py:50
  208.2 9.8 %custom-call.62 = f32[1,128,128]{1,2,0:T(8,128)S(1)} custom-call(f32[1,128,128]{2,1,0:T(8,128)S(1)} %get-tuple-element.66), custom_call_target="InvertDiagBlocksLowerTriangular" | custom-call | tf_op jit(solution)/shard_map/jit(cholesky)/cholesky | solution.py:50
  224.4 11.9 %cholesky.244 = f32[128,128]{1,0:T(8,128)S(1)} custom-call(f32[128,128]{1,0:T(8,128)S(1)} %cholesky.584), custom_call_target="Cholesky" | custom-call | tf_op jit(solution)/shard_map/jit(cholesky)/cholesky | solution.py:50
  236.9 9.8 %custom-call.63 = f32[1,128,128]{1,2,0:T(8,128)S(1)} custom-call(f32[1,128,128]{2,1,0:T(8,128)S(1)} %get-tuple-element.63), custom_call_target="InvertDiagBlocksLowerTriangular" | custom-call | tf_op jit(solution)/shard_map/jit(cholesky)/cholesky | solution.py:50
  250.1 11.7 %cholesky.468 = f32[128,128]{1,0:T(8,128)S(1)} custom-call(f32[128,128]{1,0:T(8,128)S(1)} %cholesky.589), custom_call_target="Cholesky" | custom-call | tf_op jit(solution)/shard_map/jit(cholesky)/cholesky | solution.py:50
  263.1 9.8 %custom-call.64 = f32[1,128,128]{1,2,0:T(8,128)S(1)} custom-call(f32[1,128,128]{2,1,0:T(8,128)S(1)} %get-tuple-element.60), custom_call_target="InvertDiagBlocksLowerTriangular" | custom-call | tf_op jit(solution)/shard_map/jit(cholesky)/cholesky | solution.py:50
  276.4 11.9 %cholesky.487 = f32[128,128]{1,0:T(8,128)S(1)} custom-call(f32[128,128]{1,0:T(8,128)S(1)} %cholesky.594), custom_call_target="Cholesky" | custom-call | tf_op jit(solution)/shard_map/jit(cholesky)/cholesky | solution.py:50
  289.6 9.8 %custom-call.65 = f32[1,128,128]{1,2,0:T(8,128)S(1)} custom-call(f32[1,128,128]{2,1,0:T(8,128)S(1)} %get-tuple-element.57), custom_call_target="InvertDiagBlocksLowerTriangular" | custom-call | tf_op jit(solution)/shard_map/jit(cholesky)/cholesky | solution.py:50
  302.9 11.7 %cholesky.506 = f32[128,128]{1,0:T(8,128)S(1)} custom-call(f32[128,128]{1,0:T(8,128)S(1)} %cholesky.599), custom_call_target="Cholesky" | custom-call | tf_op jit(solution)/shard_map/jit(cholesky)/cholesky | solution.py:50
  316.0 10.2 %custom-call.66 = f32[1,128,128]{1,2,0:T(8,128)S(1)} custom-call(f32[1,128,128]{2,1,0:T(8,128)S(1)} %get-tuple-element.54), custom_call_target="InvertDiagBlocksLowerTriangular" | custom-call | tf_op jit(solution)/shard_map/jit(cholesky)/cholesky | solution.py:50
  329.5 11.7 %cholesky.526 = f32[128,128]{1,0:T(8,128)S(1)} custom-call(f32[128,128]{1,0:T(8,128)S(1)} %cholesky.604), custom_call_target="Cholesky" | custom-call | tf_op jit(solution)/shard_map/jit(cholesky)/cholesky | solution.py:50
  342.5 9.8 %custom-call.67 = f32[1,128,128]{1,2,0:T(8,128)S(1)} custom-call(f32[1,128,128]{2,1,0:T(8,128)S(1)} %get-tuple-element.51), custom_call_target="InvertDiagBlocksLowerTriangular" | custom-call | tf_op jit(solution)/shard_map/jit(cholesky)/cholesky | solution.py:50
  355.3 11.9 %cholesky.546 = f32[128,128]{1,0:T(8,128)S(1)} custom-call(f32[128,128]{1,0:T(8,128)S(1)} %cholesky.609), custom_call_target="Cholesky" | custom-call | tf_op jit(solution)/shard_map/jit(cholesky)/cholesky | solution.py:50
  368.4 9.8 %custom-call.68 = f32[1,128,128]{1,2,0:T(8,128)S(1)} custom-call(f32[1,128,128]{2,1,0:T(8,128)S(1)} %get-tuple-element.48), custom_call_target="InvertDiagBlocksLowerTriangular" | custom-call | tf_op jit(solution)/shard_map/jit(cholesky)/cholesky | solution.py:50
  380.9 11.7 %cholesky.564 = f32[128,128]{1,0:T(8,128)S(1)} custom-call(f32[128,128]{1,0:T(8,128)S(1)} %convolution_subtract_fusion.13), custom_call_target="Cholesky" | custom-call | tf_op jit(solution)/shard_map/jit(cholesky)/cholesky | solution.py:50
  399.5 6.6 %fusion.1 = (f32[1024,1024]{1,0:T(8,128)}, f32[1024,1024]{1,0:T(8,128)}) fusion(f32[1024,1024]{1,0:T(8,128)} %get-tuple-element.46, pred[]{:T(512)S(6)} %cholesky.579), kind=kLoop, calls=%fused_computation.8 | loop fusion | flops 4194304 | bytes 12582913 | tf_op jit(solution)/shard_map/triangular_solve | solution.py:54
  406.2 27.3 %while.1 = (s32[]{:T(128)}, f32[1024,1024]{1,0:T(8,128)}, s32[8,2]{0,1:T(2,128)S(1)}, f32[8,128,128]{2,1,0:T(8,128)}, s32[]{:T(128)}) while((s32[]{:T(128)}, f32[1024,1024]{1,0:T(8,128)}, s32[8,2]{0,1:T(2,128)S(1)}, f32[8,128,128]{2,1,0:T(8,128)}, s32[]{:T(128)}) %tuple.61), condition=%wide.while_cond, body=%wide.while_body.sunk | while | flops 2 | bytes 132205 | solution.py:54
  433.4 79.6 %custom-call.69 = f32[8,128,128]{1,2,0:T(8,128)S(1)} custom-call(f32[8,128,128]{2,1,0:T(8,128)} %get-tuple-element.9), custom_call_target="InvertDiagBlocksLowerTriangular" | custom-call | tf_op jit(solution)/shard_map/triangular_solve | solution.py:54
  550.1 17.3 %gather_fusion.1 = f32[1024]{0:T(1024)S(1)} fusion(f32[1024,1024]{1,0:T(8,128)} %get-tuple-element.23, s32[1024]{0:T(1024)S(1)} %bitcast.159), kind=kCustom, calls=%fused_computation.1 | custom fusion | bytes 16384 | tf_op jit(solution)/shard_map/jit(diagonal)/cond/branch_0_fun/gather | solution.py:51
  (123 shorter events, 126.8 us)
Async XLA Ops:
  7.2 172.0 %all-reduce.3.cloned.1.call-start = ((), (), s32[]{:S(2)}) async-start(), calls=%async_computation | async-start | bytes 8388608 | tf_op jit(solution)/shard_map/psum | solution.py:48
  8.5 14.2 %collective-permute-start = (bf16[256,1024]{1,0:T(8,128)(2,1)S(1)}, bf16[256,1024]{1,0:T(8,128)(2,1)S(1)}, u32[]{:S(2)}, u32[]{:S(2)}) collective-permute-start(bf16[256,1024]{1,0:T(8,128)(2,1)S(1)} %get-tuple-element.26), channel_id=1, source_target_pairs={{0,1},{1,2},{2,3},{3,4},{4,5},{5,6},{6,7},{7,8},{8,9},{9,10},{10,1... | collective-permute-start | bytes 1572872 | tf_op jit(solution)/shard_map/ppermute | solution.py:17
  12.5 11.7 %collective-permute-start.1 = (bf16[256,1024]{1,0:T(8,128)(2,1)S(1)}, bf16[256,1024]{1,0:T(8,128)(2,1)S(1)}, u32[]{:S(2)}, u32[]{:S(2)}) collective-permute-start(bf16[256,1024]{1,0:T(8,128)(2,1)S(1)} %get-tuple-element.27), channel_id=1, source_target_pairs={{1,0},{2,1},{3,2},{4,3},{5,4},{6,5},{7,6},{8,7},{9,8},{10,9},{11,1... | collective-permute-start | bytes 1572872 | tf_op jit(solution)/shard_map/ppermute | solution.py:20
  31.8 3.3 copy-start.1
  194.5 1.9 copy-start
  513.0 13.8 %copy-start.3 = (f32[8,128,128]{1,2,0:T(8,128)}, f32[8,128,128]{1,2,0:T(8,128)S(1)}, u32[]{:S(2)}) copy-start(f32[8,128,128]{1,2,0:T(8,128)S(1)} %custom-call.69) | copy-start | bytes 1572868
  531.6 18.0 %copy-start.2 = (bf16[512,1024]{1,0:T(8,128)(2,1)S(1)}, bf16[512,1024]{1,0:T(8,128)(2,1)}, u32[]{:S(2)}) copy-start(bf16[512,1024]{1,0:T(8,128)(2,1)} %param.6) | copy-start | bytes 3145732
  543.5 23.9 %copy-start.4 = (f32[1,1024]{1,0:T(1,128)S(1)}, f32[1,1024]{1,0:T(1,128)}, u32[]{:S(2)}) copy-start(f32[1,1024]{1,0:T(1,128)} %param.9) | copy-start | bytes 12292
  545.5 22.6 %collective-permute-start.2 = (bf16[1,512,1024]{1,2,0:T(8,128)(2,1)}, bf16[1,512,1024]{1,2,0:T(8,128)(2,1)}, u32[]{:S(2)}, u32[]{:S(2)}) collective-permute-start(bf16[1,512,1024]{1,2,0:T(8,128)(2,1)} %fusion.9), channel_id=1, source_target_pairs={{0,16},{16,32},{32,48},{48,64},{64,80},{80,96},{96,112},{112,128},... | collective-permute-start | bytes 3145736 | tf_op jit(solution)/shard_map/ppermute | solution.py:28
Sparse Core Ops, SparseCore 0:
  35.2 143.8 all-reduce.2
where the time goes:
time: 584 us; the launch traced here: 578 us
  other arithmetic  273 us (47%)
  waiting for transfers between devices  146 us (25%)
  local copies, waits for them, and re-layouts  63.6 us (11%)
  matrix products  61.6 us (11%)
  between operations  19.7 us (3%)
  starting transfers between devices  13.7 us (2%)
    another operation x30, other arithmetic, body(): factor = jnp.linalg.cholesky(gram_matrix)  172 us
    psum x1, waiting for transfers between devices, body(): gram_matrix = lax.psum(partial_value, 'row')  144 us
    another operation x3, other arithmetic, body(): lax.linalg.triangular_solve(factor, wide_rows, left_side=False, lower=Tru...  86.2 us
    another operation x15, matrix products, body(): lax.linalg.triangular_solve(factor, wide_rows, left_side=False, lower=Tru...  31.8 us
    another operation x24, local copies, waits for them, and re-layouts  27.3 us
    another operation x14, matrix products, body(): factor = jnp.linalg.cholesky(gram_matrix)  23.1 us
    gather x1, local copies, waits for them, and re-layouts, body(): next_growth = growth + jnp.log(jnp.diagonal(factor))[None, :]  17.3 us
  transfers between devices with their start and end apart: 4, of which 3 were waited for; matrix products, arithmetic and copies ran while one was open for 4% of the time, Pallas kernels for 0%

commit v1 on v0

--- a/solution.py
+++ b/solution.py
@@ -1,11 +1,26 @@
+import functools
 import jax
 import jax.numpy as jnp
 from jax import lax
 from jax.sharding import PartitionSpec as P
+from jax.lax import axis_size, ppermute
 
 BS = 64
 NB = 4
 REACH = 4
+
+
+def match_entries_by_axis(row_data, chip_axis):
+    total_devices = axis_size(chip_axis)
+    view_out = row_data
+    for src_i in [b for b in (1, 2, 4, 8, 16) if b < total_devices]:
+        raw_out = tuple(((u, u ^ src_i) for u in range(total_devices)))
+        known = ppermute(view_out, axis_name=chip_axis, perm=raw_out)
+        view_out = view_out + known
+    return view_out
+
+
+perform_the_turns = functools.partial(match_entries_by_axis, chip_axis="row")
 
 
 def padded_2(block, sides, width):
@@ -45,7 +60,7 @@
     partial_value = lax.dot_general(
         propagated, propagated, (((0,), (0,)), ((), ())), preferred_element_type=jnp.float32
     )
-    gram_matrix = lax.psum(partial_value, "row")
+    gram_matrix = perform_the_turns(partial_value)
     gram_matrix = gram_matrix / (row_count * lax.axis_size("row"))
     factor = jnp.linalg.cholesky(gram_matrix)
     next_growth = growth + jnp.log(jnp.diagonal(factor))[None, :]

time: 584 us -> 813 us (1.39)
  waiting for transfers between devices: 146 us -> 353 us
  starting transfers between devices: 13.7 us -> 39.7 us
  between operations: 19.7 us -> 6.27 us
    ppermute x0 -> x4, waiting for transfers between devices: none -> 351 us  [match_entries_by_axis(): known = ppermute(view_out, axis_name=chip_axis, perm=raw_out)]
    psum x1 -> x0, waiting for transfers between devices: 144 us -> none  [body(): gram_matrix = lax.psum(partial_value, 'row')]
    ppermute x0 -> x4, starting transfers between devices: none -> 21.5 us  [match_entries_by_axis(): known = ppermute(view_out, axis_name=chip_axis, perm=raw_out)]
  transfers between devices with their start and end apart: 4 -> 7, of which waited for: 3 -> 6; matrix products, arithmetic and copies ran while one was open for 4% -> 3% of each run, Pallas kernels for 0% -> 0%
where the time goes in v1:
time: 813 us; the launch traced here: 803 us
  waiting for transfers between devices  353 us (43%)
  other arithmetic  281 us (35%)
  local copies, waits for them, and re-layouts  63.2 us (8%)
  matrix products  59.6 us (7%)
  starting transfers between devices  39.7 us (5%)
    ppermute x4, waiting for transfers between devices, match_entries_by_axis(): known = ppermute(view_out, axis_name=chip_axis, perm=raw_out)  351 us
    another operation x30, other arithmetic, body(): factor = jnp.linalg.cholesky(gram_matrix)  172 us
    another operation x3, other arithmetic, body(): lax.linalg.triangular_solve(factor, wide_rows, left_side=False, lower=Tru...  86.4 us
    another operation x15, matrix products, body(): lax.linalg.triangular_solve(factor, wide_rows, left_side=False, lower=Tru...  31.7 us
    another operation x24, local copies, waits for them, and re-layouts  27.3 us
    another operation x14, matrix products, body(): factor = jnp.linalg.cholesky(gram_matrix)  23 us
    ppermute x4, starting transfers between devices, match_entries_by_axis(): known = ppermute(view_out, axis_name=chip_axis, perm=raw_out)  21.5 us
    gather x1, local copies, waits for them, and re-layouts, body(): next_growth = growth + jnp.log(jnp.diagonal(factor))[None, :]  17.3 us
  transfers between devices with their start and end apart: 7, of which 6 were waited for; matrix products, arithmetic and copies ran while one was open for 3% of the time, Pallas kernels for 0%

profile of v1, /device:TPU:1, one launch (start us, length us, event | category | flops | bytes accessed | tf_op | source)
XLA Modules:
  0.0 803.0 jit_solution(18006855504516361832)
XLA Ops:
  32.5 87.2 %collective-permute-done.2 = f32[1024,1024]{0,1:T(8,128)S(1)} collective-permute-done((f32[1024,1024]{0,1:T(8,128)S(1)}, f32[1024,1024]{0,1:T(8,128)S(1)}, u32[]{:S(2)}, u32[]{:S(2)}) %collective-permute-start.2) | collective-permute-done | bytes 4194336 | tf_op jit(solution)/shard_map/ppermute | solution.py:18
  121.1 8.1 %collective-permute-start.3 = (f32[1024,1024]{0,1:T(8,128)S(1)}, f32[1024,1024]{0,1:T(8,128)S(1)}, u32[]{:S(2)}, u32[]{:S(2)}) collective-permute-start(f32[1024,1024]{0,1:T(8,128)S(1)} %add.199), channel_id=1, source_target_pairs={{0,2},{1,3},{2,0},{3,1},{4,6},{5,7},{6,4},{7,5},{8,10},{9,11},{10,... | collective-permute-start | bytes 12582920 | tf_op jit(solution)/shard_map/ppermute | solution.py:18
  129.3 88.5 %collective-permute-done.3 = f32[1024,1024]{0,1:T(8,128)S(1)} collective-permute-done((f32[1024,1024]{0,1:T(8,128)S(1)}, f32[1024,1024]{0,1:T(8,128)S(1)}, u32[]{:S(2)}, u32[]{:S(2)}) %collective-permute-start.3) | collective-permute-done | bytes 4194336 | tf_op jit(solution)/shard_map/ppermute | solution.py:18
  222.3 87.9 %collective-permute-done.4 = f32[1024,1024]{0,1:T(8,128)S(1)} collective-permute-done((f32[1024,1024]{0,1:T(8,128)S(1)}, f32[1024,1024]{0,1:T(8,128)S(1)}, u32[]{:S(2)}, u32[]{:S(2)}) %collective-permute-start.4) | collective-permute-done | bytes 4194336 | tf_op jit(solution)/shard_map/ppermute | solution.py:18
  317.8 87.3 %collective-permute-done.5 = f32[1024,1024]{0,1:T(8,128)} collective-permute-done((f32[1024,1024]{0,1:T(8,128)}, f32[1024,1024]{0,1:T(8,128)}, u32[]{:S(2)}, u32[]{:S(2)}) %collective-permute-start.5) | collective-permute-done | bytes 4194336 | tf_op jit(solution)/shard_map/ppermute | solution.py:18
  423.9 11.7 %cholesky.223 = f32[128,128]{1,0:T(8,128)S(1)} custom-call(f32[128,128]{1,0:T(8,128)S(1)} %cholesky.580), custom_call_target="Cholesky" | custom-call | tf_op jit(solution)/shard_map/jit(cholesky)/cholesky | solution.py:65
  435.6 9.8 %custom-call.62 = f32[1,128,128]{1,2,0:T(8,128)S(1)} custom-call(f32[1,128,128]{2,1,0:T(8,128)S(1)} %get-tuple-element.66), custom_call_target="InvertDiagBlocksLowerTriangular" | custom-call | tf_op jit(solution)/shard_map/jit(cholesky)/cholesky | solution.py:65
  451.9 11.9 %cholesky.244 = f32[128,128]{1,0:T(8,128)S(1)} custom-call(f32[128,128]{1,0:T(8,128)S(1)} %cholesky.584), custom_call_target="Cholesky" | custom-call | tf_op jit(solution)/shard_map/jit(cholesky)/cholesky | solution.py:65
  464.4 9.8 %custom-call.63 = f32[1,128,128]{1,2,0:T(8,128)S(1)} custom-call(f32[1,128,128]{2,1,0:T(8,128)S(1)} %get-tuple-element.63), custom_call_target="InvertDiagBlocksLowerTriangular" | custom-call | tf_op jit(solution)/shard_map/jit(cholesky)/cholesky | solution.py:65
  477.6 11.7 %cholesky.468 = f32[128,128]{1,0:T(8,128)S(1)} custom-call(f32[128,128]{1,0:T(8,128)S(1)} %cholesky.589), custom_call_target="Cholesky" | custom-call | tf_op jit(solution)/shard_map/jit(cholesky)/cholesky | solution.py:65
  490.6 9.8 %custom-call.64 = f32[1,128,128]{1,2,0:T(8,128)S(1)} custom-call(f32[1,128,128]{2,1,0:T(8,128)S(1)} %get-tuple-element.60), custom_call_target="InvertDiagBlocksLowerTriangular" | custom-call | tf_op jit(solution)/shard_map/jit(cholesky)/cholesky | solution.py:65
  503.9 12.1 %cholesky.487 = f32[128,128]{1,0:T(8,128)S(1)} custom-call(f32[128,128]{1,0:T(8,128)S(1)} %cholesky.594), custom_call_target="Cholesky" | custom-call | tf_op jit(solution)/shard_map/jit(cholesky)/cholesky | solution.py:65
  517.3 9.8 %custom-call.65 = f32[1,128,128]{1,2,0:T(8,128)S(1)} custom-call(f32[1,128,128]{2,1,0:T(8,128)S(1)} %get-tuple-element.57), custom_call_target="InvertDiagBlocksLowerTriangular" | custom-call | tf_op jit(solution)/shard_map/jit(cholesky)/cholesky | solution.py:65
  530.6 11.7 %cholesky.506 = f32[128,128]{1,0:T(8,128)S(1)} custom-call(f32[128,128]{1,0:T(8,128)S(1)} %cholesky.599), custom_call_target="Cholesky" | custom-call | tf_op jit(solution)/shard_map/jit(cholesky)/cholesky | solution.py:65
  543.7 9.9 %custom-call.66 = f32[1,128,128]{1,2,0:T(8,128)S(1)} custom-call(f32[1,128,128]{2,1,0:T(8,128)S(1)} %get-tuple-element.54), custom_call_target="InvertDiagBlocksLowerTriangular" | custom-call | tf_op jit(solution)/shard_map/jit(cholesky)/cholesky | solution.py:65
  556.9 11.7 %cholesky.526 = f32[128,128]{1,0:T(8,128)S(1)} custom-call(f32[128,128]{1,0:T(8,128)S(1)} %cholesky.604), custom_call_target="Cholesky" | custom-call | tf_op jit(solution)/shard_map/jit(cholesky)/cholesky | solution.py:65
  569.9 9.8 %custom-call.67 = f32[1,128,128]{1,2,0:T(8,128)S(1)} custom-call(f32[1,128,128]{2,1,0:T(8,128)S(1)} %get-tuple-element.51), custom_call_target="InvertDiagBlocksLowerTriangular" | custom-call | tf_op jit(solution)/shard_map/jit(cholesky)/cholesky | solution.py:65
  582.7 11.9 %cholesky.546 = f32[128,128]{1,0:T(8,128)S(1)} custom-call(f32[128,128]{1,0:T(8,128)S(1)} %cholesky.609), custom_call_target="Cholesky" | custom-call | tf_op jit(solution)/shard_map/jit(cholesky)/cholesky | solution.py:65
  595.9 9.8 %custom-call.68 = f32[1,128,128]{1,2,0:T(8,128)S(1)} custom-call(f32[1,128,128]{2,1,0:T(8,128)S(1)} %get-tuple-element.48), custom_call_target="InvertDiagBlocksLowerTriangular" | custom-call | tf_op jit(solution)/shard_map/jit(cholesky)/cholesky | solution.py:65
  608.3 11.7 %cholesky.564 = f32[128,128]{1,0:T(8,128)S(1)} custom-call(f32[128,128]{1,0:T(8,128)S(1)} %slice_subtract_fusion.6), custom_call_target="Cholesky" | custom-call | tf_op jit(solution)/shard_map/jit(cholesky)/cholesky | solution.py:65
  633.6 27.3 %while.1 = (s32[]{:T(128)}, f32[1024,1024]{1,0:T(8,128)}, s32[8,2]{0,1:T(2,128)S(1)}, f32[8,128,128]{2,1,0:T(8,128)}, s32[]{:T(128)}) while((s32[]{:T(128)}, f32[1024,1024]{1,0:T(8,128)}, s32[8,2]{0,1:T(2,128)S(1)}, f32[8,128,128]{2,1,0:T(8,128)}, s32[]{:T(128)}) %tuple.61), condition=%wide.while_cond, body=%wide.while_body.sunk | while | flops 2 | bytes 132205 | solution.py:69
  660.9 79.8 %custom-call.69 = f32[8,128,128]{1,2,0:T(8,128)S(1)} custom-call(f32[8,128,128]{2,1,0:T(8,128)} %get-tuple-element.9), custom_call_target="InvertDiagBlocksLowerTriangular" | custom-call | tf_op jit(solution)/shard_map/triangular_solve | solution.py:69
  773.0 8.6 %collective-permute-start.6 = (bf16[1,512,1024]{1,2,0:T(8,128)(2,1)}, bf16[1,512,1024]{1,2,0:T(8,128)(2,1)}, u32[]{:S(2)}, u32[]{:S(2)}) collective-permute-start(bf16[1,512,1024]{1,2,0:T(8,128)(2,1)} %fusion.9), channel_id=1, source_target_pairs={{0,16},{16,32},{32,48},{48,64},{64,80},{80,96},{96,112},{112,128},... | collective-permute-start | bytes 3145736 | tf_op jit(solution)/shard_map/ppermute | solution.py:43
  782.2 17.3 %gather_fusion.1 = f32[1024]{0:T(1024)S(1)} fusion(f32[1024,1024]{1,0:T(8,128)} %get-tuple-element.23, s32[1024]{0:T(1024)S(1)} %bitcast.161), kind=kCustom, calls=%fused_computation.1 | custom fusion | bytes 16384 | tf_op jit(solution)/shard_map/jit(diagonal)/cond/branch_0_fun/gather | solution.py:66
  (131 shorter events, 168.7 us)
Async XLA Ops:
  1.9 14.2 %collective-permute-start = (bf16[256,1024]{1,0:T(8,128)(2,1)S(1)}, bf16[256,1024]{1,0:T(8,128)(2,1)S(1)}, u32[]{:S(2)}, u32[]{:S(2)}) collective-permute-start(bf16[256,1024]{1,0:T(8,128)(2,1)S(1)} %get-tuple-element.26), channel_id=1, source_target_pairs={{0,1},{1,2},{2,3},{3,4},{4,5},{5,6},{6,7},{7,8},{8,9},{9,10},{10,1... | collective-permute-start | bytes 1572872 | tf_op jit(solution)/shard_map/ppermute | solution.py:32
  5.9 11.7 %collective-permute-start.1 = (bf16[256,1024]{1,0:T(8,128)(2,1)S(1)}, bf16[256,1024]{1,0:T(8,128)(2,1)S(1)}, u32[]{:S(2)}, u32[]{:S(2)}) collective-permute-start(bf16[256,1024]{1,0:T(8,128)(2,1)S(1)} %get-tuple-element.27), channel_id=1, source_target_pairs={{1,0},{2,1},{3,2},{4,3},{5,4},{6,5},{7,6},{8,7},{9,8},{10,9},{11,1... | collective-permute-start | bytes 1572872 | tf_op jit(solution)/shard_map/ppermute | solution.py:35
  25.2 292.3 %copy-start.1 = (bf16[8,1024,64]{1,2,0:T(8,128)(2,1)}, bf16[8,1024,64]{1,2,0:T(8,128)(2,1)S(1)}, u32[]{:S(2)}) copy-start(bf16[8,1024,64]{1,2,0:T(8,128)(2,1)S(1)} %bitcast_convert_fusion) | copy-start | bytes 3145732
  26.6 93.2 %collective-permute-start.2 = (f32[1024,1024]{0,1:T(8,128)S(1)}, f32[1024,1024]{0,1:T(8,128)S(1)}, u32[]{:S(2)}, u32[]{:S(2)}) collective-permute-start(f32[1024,1024]{0,1:T(8,128)S(1)} %convolution_bitcast_fusion), channel_id=1, source_target_pairs={{0,1},{1,0},{2,3},{3,2},{4,5},{5,4},{6,7},{7,6},{8,9},{9,8},{10,11... | collective-permute-start | bytes 12582920 | tf_op jit(solution)/shard_map/ppermute | solution.py:18
  121.1 96.7 %collective-permute-start.3 = (f32[1024,1024]{0,1:T(8,128)S(1)}, f32[1024,1024]{0,1:T(8,128)S(1)}, u32[]{:S(2)}, u32[]{:S(2)}) collective-permute-start(f32[1024,1024]{0,1:T(8,128)S(1)} %add.199), channel_id=1, source_target_pairs={{0,2},{1,3},{2,0},{3,1},{4,6},{5,7},{6,4},{7,5},{8,10},{9,11},{10,... | collective-permute-start | bytes 12582920 | tf_op jit(solution)/shard_map/ppermute | solution.py:18
  219.2 91.1 %collective-permute-start.4 = (f32[1024,1024]{0,1:T(8,128)S(1)}, f32[1024,1024]{0,1:T(8,128)S(1)}, u32[]{:S(2)}, u32[]{:S(2)}) collective-permute-start(f32[1024,1024]{0,1:T(8,128)S(1)} %add.200), channel_id=1, source_target_pairs={{0,4},{1,5},{2,6},{3,7},{4,0},{5,1},{6,2},{7,3},{8,12},{9,13},{10,... | collective-permute-start | bytes 12582920 | tf_op jit(solution)/shard_map/ppermute | solution.py:18
  313.1 92.0 %collective-permute-start.5 = (f32[1024,1024]{0,1:T(8,128)}, f32[1024,1024]{0,1:T(8,128)}, u32[]{:S(2)}, u32[]{:S(2)}) collective-permute-start(f32[1024,1024]{0,1:T(8,128)} %add.201), channel_id=1, source_target_pairs={{0,8},{1,9},{2,10},{3,11},{4,12},{5,13},{6,14},{7,15},{8,0},{9,1},... | collective-permute-start | bytes 12582920 | tf_op jit(solution)/shard_map/ppermute | solution.py:18
  421.9 1.9 copy-start
  740.7 13.8 %copy-start.3 = (f32[8,128,128]{1,2,0:T(8,128)}, f32[8,128,128]{1,2,0:T(8,128)S(1)}, u32[]{:S(2)}) copy-start(f32[8,128,128]{1,2,0:T(8,128)S(1)} %custom-call.69) | copy-start | bytes 1572868
  759.2 22.4 %copy-start.2 = (bf16[512,1024]{1,0:T(8,128)(2,1)S(1)}, bf16[512,1024]{1,0:T(8,128)(2,1)}, u32[]{:S(2)}) copy-start(bf16[512,1024]{1,0:T(8,128)(2,1)} %param.6) | copy-start | bytes 3145732
  771.1 28.4 %copy-start.4 = (f32[1,1024]{1,0:T(1,128)S(1)}, f32[1,1024]{1,0:T(1,128)}, u32[]{:S(2)}) copy-start(f32[1,1024]{1,0:T(1,128)} %param.9) | copy-start | bytes 12292
  773.0 27.1 %collective-permute-start.6 = (bf16[1,512,1024]{1,2,0:T(8,128)(2,1)}, bf16[1,512,1024]{1,2,0:T(8,128)(2,1)}, u32[]{:S(2)}, u32[]{:S(2)}) collective-permute-start(bf16[1,512,1024]{1,2,0:T(8,128)(2,1)} %fusion.9), channel_id=1, source_target_pairs={{0,16},{16,32},{32,48},{48,64},{64,80},{80,96},{96,112},{112,128},... | collective-permute-start | bytes 3145736 | tf_op jit(solution)/shard_map/ppermute | solution.py:43
